TPU v7x, 256 devices: a whole 4x4x8 slice. The times are simulated.
256 devices in a mesh: dp: 16 (over y, x), expert: 16 (over z, core).
Axes of the slice: x: 4, y: 4, z: 8, core: 2. Of those that a mesh axis runs over, the one named last changes fastest.
Arguments:
- tokens: bfloat16 [32768, 768], P(('dp', 'expert')), may hold values from -6 to 6
- cotangent: bfloat16 [32768, 768], P(('dp', 'expert')), may hold values from -6 to 6
- routes: int32 [32768, 2], P(('dp', 'expert')), may hold values from 0 to 15, all different within a row; in each aligned block of 128 rows (0 to 127, 128 to 255, ...) at most 48 rows name the same one
- gates: float32 [32768, 2], P(('dp', 'expert')), may hold values from 0.1 to 1
- w_in: bfloat16 [16, 2304, 768], P('expert', 'dp'), may hold values from -0.21875 to 0.21875
- w_out: bfloat16 [16, 2304, 768], P('expert', 'dp'), may hold values from -0.125 to 0.125
Outputs:
- d_tokens: bfloat16 [32768, 768], P(('dp', 'expert'))
- grad_in: float32 [16, 2304, 768], P('expert', 'dp')
- grad_out: float32 [16, 2304, 768], P('expert', 'dp')
Inputs may be any that keep to these rules, and one draw needn't show every extreme that they name: `routes`: within the rows of one device (128 rows) no expert is named more than 48 times, and in every draw some expert is named exactly 48 times by the rows of some device; the 2 entries of a row differ.
All inputs are finite; a program needn't handle non-finite values.
Results may differ from a plain program's by a relative error of at most 0.015.
Values may be sent and summed in bfloat16 or wider, within the bound.
No kernel may reach another device: no remote copies, remote signals or barrier semaphores. Data moves between devices by JAX's collectives and lax.ppermute only.
A program may use at most 64 MiB of HBM per device.

v0:
```python
import jax
import jax.numpy as jnp
from jax import lax
from jax.sharding import PartitionSpec as P

tanh_coef = 0.7978845608028654
cubic_coef = 0.044715


def gelu_tanh(value):
    inner = tanh_coef * (value + cubic_coef * value * value * value)
    return 0.5 * value * (1.0 + jnp.tanh(inner))


def gelu_slope(value):
    inner = tanh_coef * (value + cubic_coef * value * value * value)
    slope_t = jnp.tanh(inner)
    return 0.5 * (1.0 + slope_t) + 0.5 * value * (1.0 - slope_t * slope_t) * tanh_coef * (
        1.0 + 3.0 * cubic_coef * value * value
    )


def dispatch_tables(route_blk, gate_blk, experts, capacity):
    tok_rows = route_blk.shape[0]
    flat = route_blk.reshape(-1)
    onehot = (flat[:, None] == jnp.arange(experts, dtype=jnp.int32)[None, :]).astype(jnp.int32)
    before = jnp.cumsum(onehot, axis=0) - onehot
    position = jnp.sum(before * onehot, axis=1)
    slots = (flat * capacity + position).reshape(tok_rows, -1)
    slot_ids = jnp.arange(experts * capacity, dtype=jnp.int32)
    placed = slot_ids[:, None, None] == slots[None, :, :]
    route_mat = jnp.sum(placed.astype(jnp.int32), axis=2).astype(jnp.bfloat16)
    gate_slot = jnp.sum(jnp.where(placed, gate_blk[None, :, :], jnp.float32(0.0)), axis=(1, 2))
    return (route_mat, gate_slot)


def shards(tokens, cotangent, routes, gates, w_in, w_out):
    experts = lax.axis_size("expert")
    tok_rows, model_width = tokens.shape
    top_count = routes.shape[1]
    capacity = 3 * tok_rows * top_count // experts
    shard_rows = w_in.shape[1]
    slot_rows = experts * capacity
    route_mat, gate_slot = dispatch_tables(routes, gates, experts, capacity)
    rows_sent = jnp.dot(route_mat, tokens, preferred_element_type=jnp.float32).astype(jnp.bfloat16)
    grad_rows = jnp.dot(route_mat, cotangent, preferred_element_type=jnp.float32)
    grads_sent = (gate_slot[:, None] * grad_rows).astype(jnp.bfloat16)
    rows_recv, grads_recv = (
        lax.all_to_all(
            rows_sent.reshape(experts, capacity, model_width),
            "expert",
            split_axis=0,
            concat_axis=0,
            tiled=True,
        ),
        lax.all_to_all(
            grads_sent.reshape(experts, capacity, model_width),
            "expert",
            split_axis=0,
            concat_axis=0,
            tiled=True,
        ),
    )
    rows_in = rows_recv.reshape(slot_rows, model_width)
    grads_in = grads_recv.reshape(slot_rows, model_width)
    piece_in = lax.all_gather(w_in[0], "dp", axis=0, tiled=True)
    piece_out = lax.all_gather(w_out[0], "dp", axis=0, tiled=True)
    pre = lax.dot_general(
        rows_in, piece_in, (((1,), (1,)), ((), ())), preferred_element_type=jnp.float32
    )
    acts = gelu_tanh(pre).astype(jnp.bfloat16)
    grad_act = lax.dot_general(
        grads_in, piece_out, (((1,), (1,)), ((), ())), preferred_element_type=jnp.float32
    )
    dpre = (grad_act * gelu_slope(pre)).astype(jnp.bfloat16)
    slot_sum = jnp.dot(dpre, piece_in, preferred_element_type=jnp.float32)
    slot_sum, acts_all, dpre_all = (slot_sum, acts, dpre)
    returned = lax.all_to_all(
        slot_sum.astype(jnp.bfloat16).reshape(experts, capacity, model_width),
        "expert",
        split_axis=0,
        concat_axis=0,
        tiled=True,
    )
    token_grads = lax.dot_general(
        route_mat,
        returned.reshape(slot_rows, model_width),
        (((0,), (0,)), ((), ())),
        preferred_element_type=jnp.float32,
    )
    d_tokens = token_grads.astype(jnp.bfloat16)
    term_in = lax.dot_general(
        dpre_all, rows_in, (((0,), (0,)), ((), ())), preferred_element_type=jnp.float32
    )
    term_out = lax.dot_general(
        acts_all, grads_in, (((0,), (0,)), ((), ())), preferred_element_type=jnp.float32
    )
    summed = lax.psum(
        jnp.concatenate([term_in, term_out], axis=1).astype(jnp.bfloat16), "dp"
    ).astype(jnp.float32)
    own_rows = lax.dynamic_slice_in_dim(summed, lax.axis_index("dp") * shard_rows, shard_rows, 0)
    grad_in = own_rows[:, :model_width][None]
    grad_out = own_rows[:, model_width:][None]
    return (d_tokens, grad_in, grad_out)


def solution(mesh):
    in_specs = (
        P(("dp", "expert"), None),
        P(("dp", "expert"), None),
        P(("dp", "expert"), None),
        P(("dp", "expert"), None),
        P("expert", "dp", None),
        P("expert", "dp", None),
    )
    out_specs = (P(("dp", "expert"), None), P("expert", "dp", None), P("expert", "dp", None))
    return jax.shard_map(shards, mesh=mesh, in_specs=in_specs, out_specs=out_specs, check_vma=False)
```

profile of v0, /device:TPU:1, one launch (start us, length us, event | category | flops | bytes accessed | tf_op | source)
XLA Modules:
  0.0 294.6 jit_solution(5425610005325512928)
XLA Ops:
  7.2 0.7 all-gather.7.cloned.1.call-update
  8.0 0.7 all-gather.5.cloned.1.call-update
  8.7 0.8 copy.29
  9.6 0.1 eq.43
  9.8 0.6 reduce-window.6
  10.4 0.2 slice_reduce_fusion
  10.7 0.1 reduce_sum.30
  10.9 0.7 multiply_add_fusion.1
  11.7 1.5 convolution_convert_fusion.2
  13.2 10.0 %all-to-all-start.1 = ((bf16[16,48,768]{2,1,0:T(8,128)(2,1)}), bf16[16,48,768]{2,1,0:T(8,128)(2,1)S(1)}, u32[]{:S(2)}, u32[]{:S(2)}) async-start(bf16[16,48,768]{2,1,0:T(8,128)(2,1)} %bitcast.4), calls=%async_computation.1 | async-start | bytes 2359296 | tf_op jit(solution)/shard_map/all_to_all | solution.py:49
  23.2 0.2 select_reduce_fusion
  23.4 1.5 multiply_convert_fusion.2
  24.9 28.9 %all-to-all-done.1 = bf16[16,48,768]{2,1,0:T(8,128)(2,1)S(1)} async-done(((bf16[16,48,768]{2,1,0:T(8,128)(2,1)}), bf16[16,48,768]{2,1,0:T(8,128)(2,1)S(1)}, u32[]{:S(2)}, u32[]{:S(2)}) %all-to-all-start.1) | async-done | bytes 1179680 | tf_op jit(solution)/shard_map/all_to_all | solution.py:49
  53.8 3.7 %all-to-all-start = ((bf16[16,48,768]{2,1,0:T(8,128)(2,1)}), bf16[16,48,768]{2,1,0:T(8,128)(2,1)S(1)}, u32[]{:S(2)}, u32[]{:S(2)}) async-start(bf16[16,48,768]{2,1,0:T(8,128)(2,1)} %bitcast.1), calls=%async_computation | async-start | bytes 2359296 | tf_op jit(solution)/shard_map/all_to_all | solution.py:56
  57.5 0.2 all-reduce.2.cloned.1.call-start
  57.7 10.5 %all-gather.7.cloned.1.call-done = bf16[1,2304,768]{2,1,0:T(8,128)(2,1)} async-done(((bf16[1,144,768]{2,1,0:T(8,128)(2,1)}), bf16[1,2304,768]{2,1,0:T(8,128)(2,1)}) %all-gather.7.cloned.1.call-update) | async-done | bytes 3538960 | tf_op jit(solution)/shard_map/all_gather | solution.py:66
  68.2 7.0 %fusion.9 = f32[768,2304]{1,0:T(8,128)} fusion(bf16[768,768]{1,0:T(8,128)(2,1)S(1)} %bitcast.49, bf16[1,2304,768]{2,1,0:T(8,128)(2,1)} %all-gather.7.cloned.1.call-done), kind=kOutput, calls=%fused_computation.15 | convolution fusion | flops 2717908992 | bytes 11796480 | tf_op jit(solution)/shard_map/dot_general | solution.py:68
  75.2 12.9 %all-to-all-done = bf16[16,48,768]{2,1,0:T(8,128)(2,1)S(1)} async-done(((bf16[16,48,768]{2,1,0:T(8,128)(2,1)}), bf16[16,48,768]{2,1,0:T(8,128)(2,1)S(1)}, u32[]{:S(2)}, u32[]{:S(2)}) %all-to-all-start) | async-done | bytes 1179680 | tf_op jit(solution)/shard_map/all_to_all | solution.py:56
  88.0 8.3 %convolution_convert_fusion = bf16[2304,768]{0,1:T(8,128)(2,1)} fusion(bf16[768,768]{1,0:T(8,128)(2,1)S(1)} %bitcast.51, f32[768,2304]{1,0:T(8,128)} %fusion.9), kind=kOutput, calls=%fused_computation.11 | convolution fusion | flops 2735603712 | bytes 11796480 | tf_op jit(solution)/shard_map/dot_general | solution.py:95
  96.4 27.6 %all-gather.5.cloned.1.call-done = bf16[1,2304,768]{2,1,0:T(8,128)(2,1)} async-done(((bf16[1,144,768]{2,1,0:T(8,128)(2,1)}), bf16[1,2304,768]{2,1,0:T(8,128)(2,1)}) %all-gather.5.cloned.1.call-update) | async-done | bytes 3538960 | tf_op jit(solution)/shard_map/all_gather | solution.py:67
  124.0 8.4 %fusion.6 = bf16[768,2304]{1,0:T(8,128)(2,1)S(1)} fusion(f32[768,2304]{1,0:T(8,128)} %fusion.9, bf16[768,768]{1,0:T(8,128)(2,1)S(1)} %bitcast.52, bf16[1,2304,768]{2,1,0:T(8,128)(2,1)} %all-gather.5.cloned.1.call-done), kind=kOutput, calls=%fused_computation.8 | convolution fusion | flops 2751528960 | bytes 15335424 | tf_op jit(solution)/shard_map/dot_general | solution.py:72
  132.5 1.7 copy-done.3
  134.2 4.7 %convolution_convert_fusion.1 = bf16[2304,768]{0,1:T(8,128)(2,1)} fusion(bf16[768,2304]{1,0:T(8,128)(2,1)S(1)} %fusion.6, bf16[768,768]{1,0:T(8,128)(2,1)S(1)} %bitcast.50), kind=kOutput, calls=%fused_computation.12 | convolution fusion | flops 2719678464 | bytes 8257536 | tf_op jit(solution)/shard_map/dot_general | solution.py:92
  138.9 6.4 %pad_maximum_fusion = bf16[2304,1536]{0,1:T(8,128)(2,1)} fusion(bf16[2304,768]{0,1:T(8,128)(2,1)} %convolution_convert_fusion, bf16[2304,768]{0,1:T(8,128)(2,1)} %convolution_convert_fusion.1), kind=kLoop, calls=%fused_computation.9 | loop fusion | flops 14155776 | bytes 14155776 | tf_op jit(solution)/shard_map/concatenate | solution.py:99
  145.3 7.0 %fusion.16 = bf16[768,768]{1,0:T(8,128)(2,1)} fusion(bf16[768,2304]{1,0:T(8,128)(2,1)} %copy-done.3, bf16[1,2304,768]{2,1,0:T(8,128)(2,1)} %all-gather.7.cloned.1.call-done), kind=kOutput, calls=%fused_computation.23 | convolution fusion | flops 2718498816 | bytes 8257536 | tf_op jit(solution)/shard_map/dot_general | solution.py:76
  152.3 8.1 %all-to-all-start.2 = ((bf16[16,48,768]{2,1,0:T(8,128)(2,1)}), bf16[16,48,768]{2,1,0:T(8,128)(2,1)S(1)}, u32[]{:S(2)}, u32[]{:S(2)}) async-start(bf16[16,48,768]{2,1,0:T(8,128)(2,1)} %bitcast.7), calls=%async_computation.2 | async-start | bytes 2359296 | tf_op jit(solution)/shard_map/all_to_all | solution.py:78
  160.4 30.6 %all-to-all-done.2 = bf16[16,48,768]{2,1,0:T(8,128)(2,1)S(1)} async-done(((bf16[16,48,768]{2,1,0:T(8,128)(2,1)}), bf16[16,48,768]{2,1,0:T(8,128)(2,1)S(1)}, u32[]{:S(2)}, u32[]{:S(2)}) %all-to-all-start.2) | async-done | bytes 1179680 | tf_op jit(solution)/shard_map/all_to_all | solution.py:78
  191.0 1.0 convolution_convert_fusion.3
  192.0 92.4 %all-reduce.2.cloned.1.call-done = bf16[2304,1536]{0,1:T(8,128)(2,1)} async-done(((bf16[2304,1536]{0,1:T(8,128)(2,1)}), bf16[2304,1536]{0,1:T(8,128)(2,1)}) %all-reduce.2.cloned.1.call-update) | async-done | bytes 7077904 | tf_op jit(solution)/shard_map/psum | solution.py:98
  284.4 1.6 dynamic-slice_convert_fusion
  286.0 1.0 copy.33
  287.0 1.0 copy.34
  (18 shorter events, 0.7 us)
Async XLA Ops:
  7.2 4.5 %copy-start = (bf16[128,768]{1,0:T(8,128)(2,1)S(1)}, bf16[128,768]{1,0:T(8,128)(2,1)}, u32[]{:S(2)}) copy-start(bf16[128,768]{1,0:T(8,128)(2,1)} %param.6) | copy-start | bytes 589828
  7.2 16.0 %copy-start.2 = (f32[128,2]{0,1:T(2,128)S(1)}, f32[128,2]{0,1:T(2,128)}, u32[]{:S(2)}) copy-start(f32[128,2]{0,1:T(2,128)} %param.9) | copy-start | bytes 3076
  7.2 16.2 %copy-start.1 = (bf16[128,768]{1,0:T(8,128)(2,1)S(1)}, bf16[128,768]{1,0:T(8,128)(2,1)}, u32[]{:S(2)}) copy-start(bf16[128,768]{1,0:T(8,128)(2,1)} %param.7) | copy-start | bytes 589828
  7.2 61.0 %all-gather.7.cloned.1.call-start = ((), (), s32[]{:S(2)}) async-start(), calls=%async_computation.5 | async-start | bytes 3760128 | tf_op jit(solution)/shard_map/all_gather | solution.py:66
  7.9 116.1 %all-gather.5.cloned.1.call-start = ((), (), s32[]{:S(2)}) async-start(), calls=%async_computation.4 | async-start | bytes 3760128 | tf_op jit(solution)/shard_map/all_gather | solution.py:67
  13.2 40.5 %all-to-all-start.1 = ((bf16[16,48,768]{2,1,0:T(8,128)(2,1)}), bf16[16,48,768]{2,1,0:T(8,128)(2,1)S(1)}, u32[]{:S(2)}, u32[]{:S(2)}) async-start(bf16[16,48,768]{2,1,0:T(8,128)(2,1)} %bitcast.4), calls=%async_computation.1 | async-start | bytes 2359296 | tf_op jit(solution)/shard_map/all_to_all | solution.py:49
  53.8 34.3 %all-to-all-start = ((bf16[16,48,768]{2,1,0:T(8,128)(2,1)}), bf16[16,48,768]{2,1,0:T(8,128)(2,1)S(1)}, u32[]{:S(2)}, u32[]{:S(2)}) async-start(bf16[16,48,768]{2,1,0:T(8,128)(2,1)} %bitcast.1), calls=%async_computation | async-start | bytes 2359296 | tf_op jit(solution)/shard_map/all_to_all | solution.py:56
  57.5 226.9 %all-reduce.2.cloned.1.call-start = ((), (), s32[]{:S(2)}) async-start(), calls=%async_computation.3 | async-start | bytes 14155776 | tf_op jit(solution)/shard_map/psum | solution.py:98
  132.4 1.8 copy-start.3
  152.3 38.6 %all-to-all-start.2 = ((bf16[16,48,768]{2,1,0:T(8,128)(2,1)}), bf16[16,48,768]{2,1,0:T(8,128)(2,1)S(1)}, u32[]{:S(2)}, u32[]{:S(2)}) async-start(bf16[16,48,768]{2,1,0:T(8,128)(2,1)} %bitcast.7), calls=%async_computation.2 | async-start | bytes 2359296 | tf_op jit(solution)/shard_map/all_to_all | solution.py:78
Sparse Core Ops, SparseCore 0:
  10.5 57.6 all-gather.6
  70.6 53.3 all-gather.4
  145.5 138.8 all-reduce.1
where the time goes:
time: 295 us
  waiting for transfers between devices  204 us (69%)
  matrix products  39.5 us (13%)
  starting transfers between devices  22 us (7%)
  between operations  13.8 us (5%)
  other arithmetic  9.72 us (3%)
  local copies, waits for them, and re-layouts  5.32 us (2%)
    psum x1, waiting for transfers between devices, shards(): lax.psum(jnp.concatenate([term_in, term_out], axis=1).astype(jnp.bfloat16...  92.4 us
    all_to_all x1, waiting for transfers between devices, shards(): lax.all_to_all(slot_sum.astype(jnp.bfloat16).reshape(experts, capacity, m...  30.6 us
    all_to_all x1, waiting for transfers between devices, shards(): lax.all_to_all(rows_sent.reshape(experts, capacity, model_width), 'expert...  28.9 us
    all_gather x1, waiting for transfers between devices, shards(): piece_out = lax.all_gather(w_out[0], 'dp', axis=0, tiled=True)  27.6 us
    all_to_all x1, waiting for transfers between devices, shards(): lax.all_to_all(grads_sent.reshape(experts, capacity, model_width), 'exper...  12.9 us
    all_gather x1, waiting for transfers between devices, shards(): piece_in = lax.all_gather(w_in[0], 'dp', axis=0, tiled=True)  10.5 us
    all_to_all x1, starting transfers between devices, shards(): lax.all_to_all(rows_sent.reshape(experts, capacity, model_width), 'expert...  9.98 us
    dot_general x1, matrix products, shards(): lax.dot_general(grads_in, piece_out, (((1,), (1,)), ((), ())), preferred_...  8.45 us
  transfers between devices with their start and end apart: 6, of which 6 were waited for; matrix products, arithmetic and copies ran while one was open for 10% of the time, Pallas kernels for 0%

commit v1 on v0

--- a/solution.py
+++ b/solution.py
@@ -64,7 +64,9 @@
     rows_in = rows_recv.reshape(slot_rows, model_width)
     grads_in = grads_recv.reshape(slot_rows, model_width)
     piece_in = lax.all_gather(w_in[0], "dp", axis=0, tiled=True)
-    piece_out = lax.all_gather(w_out[0], "dp", axis=0, tiled=True)
+    piece_out = jnp.concatenate(
+        lax.all_to_all(jnp.stack([w_out[0]] * lax.axis_size("dp")), "dp", 0, 0), axis=0
+    )
     pre = lax.dot_general(
         rows_in, piece_in, (((1,), (1,)), ((), ())), preferred_element_type=jnp.float32
     )

time: 295 us -> 318 us (1.078)
  blocking collectives: 0 us -> 35.1 us
  waiting for transfers between devices: 204 us -> 193 us
  matrix products: 39.5 us -> 33.4 us
  local copies, waits for them, and re-layouts: 5.32 us -> 10.2 us
    all_to_all x0 -> x1, blocking collectives: none -> 35.1 us  [shards(): lax.all_to_all(rows_sent.reshape(experts, capacity, model_width), 'expert...]
    all_gather x1 -> x0, waiting for transfers between devices: 27.6 us -> none  [shards(): piece_out = lax.all_gather(w_out[0], 'dp', axis=0, tiled=True)]
    all_to_all x1, waiting for transfers between devices: 12.9 us -> 30.1 us  [shards(): lax.all_to_all(grads_sent.reshape(experts, capacity, model_width), 'exper...]
    all_to_all x1, waiting for transfers between devices: 28.9 us -> 41.2 us  [shards(): lax.all_to_all(jnp.stack([w_out[0]] * lax.axis_size('dp')), 'dp', 0, 0)]
    all_gather x1, waiting for transfers between devices: 10.5 us -> 0.02 us  [shards(): piece_in = lax.all_gather(w_in[0], 'dp', axis=0, tiled=True)]
    all_to_all x1, starting transfers between devices: 3.7 us -> 10.1 us  [shards(): lax.all_to_all(grads_sent.reshape(experts, capacity, model_width), 'exper...]
    all_to_all x1, starting transfers between devices: 8.06 us -> 4.35 us  [shards(): lax.all_to_all(slot_sum.astype(jnp.bfloat16).reshape(experts, capacity, m...]
    unnamed x11 -> x19, local copies, waits for them, and re-layouts: 4.55 us -> 7.48 us
  transfers between devices with their start and end apart: 6 -> 5, of which waited for: 6 -> 4; matrix products, arithmetic and copies ran while one was open for 10% -> 8% of each run, Pallas kernels for 0% -> 0%
where the time goes in v1:
time: 318 us; the launch traced here: 317 us
  waiting for transfers between devices  193 us (61%)
  blocking collectives  35.1 us (11%)
  matrix products  33.4 us (11%)
  starting transfers between devices  21.6 us (7%)
  between operations  14.2 us (4%)
  local copies, waits for them, and re-layouts  10.2 us (3%)
  other arithmetic  9.31 us (3%)
    psum x1, waiting for transfers between devices, shards(): lax.psum(jnp.concatenate([term_in, term_out], axis=1).astype(jnp.bfloat16...  90.7 us
    all_to_all x1, waiting for transfers between devices, shards(): lax.all_to_all(jnp.stack([w_out[0]] * lax.axis_size('dp')), 'dp', 0, 0)  41.2 us
    all_to_all x1, blocking collectives, shards(): lax.all_to_all(rows_sent.reshape(experts, capacity, model_width), 'expert...  35.1 us
    all_to_all x1, waiting for transfers between devices, shards(): lax.all_to_all(slot_sum.astype(jnp.bfloat16).reshape(experts, capacity, m...  30.6 us
    all_to_all x1, waiting for transfers between devices, shards(): lax.all_to_all(grads_sent.reshape(experts, capacity, model_width), 'exper...  30.1 us
    all_to_all x1, starting transfers between devices, shards(): lax.all_to_all(grads_sent.reshape(experts, capacity, model_width), 'exper...  10.1 us
    dot_general x1, matrix products, shards(): lax.dot_general(grads_in, piece_out, (((1,), (1,)), ((), ())), preferred_...  8.45 us
    unnamed x19, local copies, waits for them, and re-layouts  7.48 us
  transfers between devices with their start and end apart: 5, of which 4 were waited for; matrix products, arithmetic and copies ran while one was open for 8% of the time, Pallas kernels for 0%

profile of v1, /device:TPU:1, one launch (start us, length us, event | category | flops | bytes accessed | tf_op | source)
XLA Modules:
  0.0 317.2 jit_solution(10296061607794248278)
XLA Ops:
  7.2 0.7 all-gather.3.cloned.1.call-update
  7.9 0.8 copy.29
  8.9 0.1 eq.39
  9.0 0.6 reduce-window.6
  9.6 0.2 slice_reduce_fusion
  9.9 0.1 reduce_sum.30
  10.1 0.7 multiply_add_fusion.1
  10.9 0.9 select_reduce_fusion
  11.8 1.5 multiply_convert_fusion.2
  13.3 10.1 %all-to-all-start = ((bf16[16,48,768]{2,1,0:T(8,128)(2,1)}), bf16[16,48,768]{2,1,0:T(8,128)(2,1)S(1)}, u32[]{:S(2)}, u32[]{:S(2)}) async-start(bf16[16,48,768]{2,1,0:T(8,128)(2,1)} %bitcast.1), calls=%async_computation | async-start | bytes 2359296 | tf_op jit(solution)/shard_map/all_to_all | solution.py:56
  23.4 0.4 convolution_convert_fusion.2
  23.9 30.1 %all-to-all-done = bf16[16,48,768]{2,1,0:T(8,128)(2,1)S(1)} async-done(((bf16[16,48,768]{2,1,0:T(8,128)(2,1)}), bf16[16,48,768]{2,1,0:T(8,128)(2,1)S(1)}, u32[]{:S(2)}, u32[]{:S(2)}) %all-to-all-start) | async-done | bytes 1179680 | tf_op jit(solution)/shard_map/all_to_all | solution.py:56
  54.0 35.1 %all_to_all.20 = bf16[16,48,768]{2,1,0:T(8,128)(2,1)} all-to-all(bf16[16,48,768]{2,1,0:T(8,128)(2,1)S(1)} %bitcast.49), channel_id=1, replica_groups=mesh['dp'=16,'expert'=16] {'expert'}, dimensions={0} | all-to-all | bytes 2359296 | tf_op jit(solution)/shard_map/all_to_all | solution.py:49
  89.0 2.0 stack.3
  91.0 6.9 %all-to-all-start.1 = ((bf16[16,144,768]{2,1,0:T(8,128)(2,1)}), bf16[16,144,768]{2,1,0:T(8,128)(2,1)}, u32[]{:S(2)}, u32[]{:S(2)}) async-start(bf16[16,144,768]{2,1,0:T(8,128)(2,1)} %stack.3), calls=%async_computation.1 | async-start | bytes 7077888 | tf_op jit(solution)/shard_map/all_to_all | solution.py:68
  98.0 0.2 all-reduce.2.cloned.1.call-start
  98.2 4.9 %fusion.9 = f32[768,2304]{1,0:T(8,128)S(1)} fusion(bf16[768,768]{1,0:T(8,128)(2,1)S(1)} %bitcast.52, bf16[1,2304,768]{2,1,0:T(8,128)(2,1)} %all-gather.3.cloned.1.call-done), kind=kOutput, calls=%fused_computation.15 | convolution fusion | flops 2717908992 | bytes 11796480 | tf_op jit(solution)/shard_map/dot_general | solution.py:70
  103.2 2.9 copy-done.6
  106.1 5.4 %convolution_convert_fusion = bf16[2304,768]{0,1:T(8,128)(2,1)} fusion(bf16[768,768]{1,0:T(8,128)(2,1)S(1)} %bitcast.50, f32[768,2304]{1,0:T(8,128)S(1)} %fusion.9), kind=kOutput, calls=%fused_computation.11 | convolution fusion | flops 2735603712 | bytes 11796480 | tf_op jit(solution)/shard_map/dot_general | solution.py:97
  111.5 41.2 %all-to-all-done.1 = bf16[16,144,768]{2,1,0:T(8,128)(2,1)} async-done(((bf16[16,144,768]{2,1,0:T(8,128)(2,1)}), bf16[16,144,768]{2,1,0:T(8,128)(2,1)}, u32[]{:S(2)}, u32[]{:S(2)}) %all-to-all-start.1) | async-done | bytes 3538976 | tf_op jit(solution)/shard_map/all_to_all | solution.py:68
  152.6 8.5 %fusion.6 = bf16[768,2304]{1,0:T(8,128)(2,1)S(1)} fusion(f32[768,2304]{1,0:T(8,128)} %copy-done.6, bf16[768,768]{1,0:T(8,128)(2,1)S(1)} %bitcast.51, bf16[2304,768]{1,0:T(8,128)(2,1)} %bitcast.4), kind=kOutput, calls=%fused_computation.8 | convolution fusion | flops 2751528960 | bytes 15335424 | tf_op jit(solution)/shard_map/dot_general | solution.py:74
  161.1 1.8 copy-done.7
  162.9 4.7 %convolution_convert_fusion.1 = bf16[2304,768]{0,1:T(8,128)(2,1)} fusion(bf16[768,2304]{1,0:T(8,128)(2,1)S(1)} %fusion.6, bf16[768,768]{1,0:T(8,128)(2,1)S(1)} %bitcast.53), kind=kOutput, calls=%fused_computation.12 | convolution fusion | flops 2719678464 | bytes 8257536 | tf_op jit(solution)/shard_map/dot_general | solution.py:94
  167.5 5.4 %pad_maximum_fusion = bf16[2304,1536]{0,1:T(8,128)(2,1)} fusion(bf16[2304,768]{0,1:T(8,128)(2,1)S(1)} %copy-done.1, bf16[2304,768]{0,1:T(8,128)(2,1)} %convolution_convert_fusion.1), kind=kLoop, calls=%fused_computation.9 | loop fusion | flops 14155776 | bytes 14155776 | tf_op jit(solution)/shard_map/concatenate | solution.py:101
  172.9 7.0 %fusion.15 = bf16[768,768]{1,0:T(8,128)(2,1)} fusion(bf16[768,2304]{1,0:T(8,128)(2,1)} %copy-done.7, bf16[1,2304,768]{2,1,0:T(8,128)(2,1)} %all-gather.3.cloned.1.call-done), kind=kOutput, calls=%fused_computation.22 | convolution fusion | flops 2718498816 | bytes 8257536 | tf_op jit(solution)/shard_map/dot_general | solution.py:78
  180.0 4.3 %all-to-all-start.3 = ((bf16[16,48,768]{2,1,0:T(8,128)(2,1)}), bf16[16,48,768]{2,1,0:T(8,128)(2,1)S(1)}, u32[]{:S(2)}, u32[]{:S(2)}) async-start(bf16[16,48,768]{2,1,0:T(8,128)(2,1)} %bitcast.8), calls=%async_computation.3 | async-start | bytes 2359296 | tf_op jit(solution)/shard_map/all_to_all | solution.py:80
  184.3 30.6 %all-to-all-done.3 = bf16[16,48,768]{2,1,0:T(8,128)(2,1)S(1)} async-done(((bf16[16,48,768]{2,1,0:T(8,128)(2,1)}), bf16[16,48,768]{2,1,0:T(8,128)(2,1)S(1)}, u32[]{:S(2)}, u32[]{:S(2)}) %all-to-all-start.3) | async-done | bytes 1179680 | tf_op jit(solution)/shard_map/all_to_all | solution.py:80
  214.9 1.0 convolution_convert_fusion.3
  215.9 90.7 %all-reduce.2.cloned.1.call-done = bf16[2304,1536]{0,1:T(8,128)(2,1)} async-done(((bf16[2304,1536]{0,1:T(8,128)(2,1)}), bf16[2304,1536]{0,1:T(8,128)(2,1)}) %all-reduce.2.cloned.1.call-update) | async-done | bytes 7077904 | tf_op jit(solution)/shard_map/psum | solution.py:100
  306.7 1.6 dynamic-slice_convert_fusion
  308.3 1.0 copy.34
  309.3 1.0 copy.33
  (25 shorter events, 0.6 us)
Async XLA Ops:
  7.2 4.6 %copy-start = (bf16[128,768]{1,0:T(8,128)(2,1)S(1)}, bf16[128,768]{1,0:T(8,128)(2,1)}, u32[]{:S(2)}) copy-start(bf16[128,768]{1,0:T(8,128)(2,1)} %param.7) | copy-start | bytes 589828
  7.2 16.2 %copy-start.5 = (bf16[128,768]{1,0:T(8,128)(2,1)S(1)}, bf16[128,768]{1,0:T(8,128)(2,1)}, u32[]{:S(2)}) copy-start(bf16[128,768]{1,0:T(8,128)(2,1)} %param.6) | copy-start | bytes 589828
  7.2 91.0 %all-gather.3.cloned.1.call-start = ((), (), s32[]{:S(2)}) async-start(), calls=%async_computation.5 | async-start | bytes 3760128 | tf_op jit(solution)/shard_map/all_gather | solution.py:66
  13.3 75.7 %copy-start.4 = (bf16[1,144,768]{2,1,0:T(8,128)(2,1)S(1)}, bf16[1,144,768]{2,1,0:T(8,128)(2,1)}, u32[]{:S(2)}) copy-start(bf16[1,144,768]{2,1,0:T(8,128)(2,1)} %param.11) | copy-start | bytes 663556
  13.3 40.7 %all-to-all-start = ((bf16[16,48,768]{2,1,0:T(8,128)(2,1)}), bf16[16,48,768]{2,1,0:T(8,128)(2,1)S(1)}, u32[]{:S(2)}, u32[]{:S(2)}) async-start(bf16[16,48,768]{2,1,0:T(8,128)(2,1)} %bitcast.1), calls=%async_computation | async-start | bytes 2359296 | tf_op jit(solution)/shard_map/all_to_all | solution.py:56
  91.0 7.2 %copy-start.2 = (bf16[16,48,768]{2,1,0:T(8,128)(2,1)S(1)}, bf16[16,48,768]{2,1,0:T(8,128)(2,1)}, u32[]{:S(2)}) copy-start(bf16[16,48,768]{2,1,0:T(8,128)(2,1)} %all_to_all.20) | copy-start | bytes 3538948
  91.0 61.6 %all-to-all-start.1 = ((bf16[16,144,768]{2,1,0:T(8,128)(2,1)}), bf16[16,144,768]{2,1,0:T(8,128)(2,1)}, u32[]{:S(2)}, u32[]{:S(2)}) async-start(bf16[16,144,768]{2,1,0:T(8,128)(2,1)} %stack.3), calls=%async_computation.1 | async-start | bytes 7077888 | tf_op jit(solution)/shard_map/all_to_all | solution.py:68
  98.0 208.7 %all-reduce.2.cloned.1.call-start = ((), (), s32[]{:S(2)}) async-start(), calls=%async_computation.4 | async-start | bytes 14155776 | tf_op jit(solution)/shard_map/psum | solution.py:100
  103.2 2.9 copy-start.6
  152.6 10.2 %copy-start.3 = (bf16[16,48,768]{2,1,0:T(8,128)(2,1)S(1)}, bf16[16,48,768]{2,1,0:T(8,128)(2,1)}, u32[]{:S(2)}) copy-start(bf16[16,48,768]{2,1,0:T(8,128)(2,1)} %all_to_all.20) | copy-start | bytes 3538948
  161.1 1.8 copy-start.7
  162.8 4.7 %copy-start.1 = (bf16[2304,768]{0,1:T(8,128)(2,1)S(1)}, bf16[2304,768]{0,1:T(8,128)(2,1)}, u32[]{:S(2)}) copy-start(bf16[2304,768]{0,1:T(8,128)(2,1)} %convolution_convert_fusion) | copy-start | bytes 10616836
  180.0 35.0 %all-to-all-start.3 = ((bf16[16,48,768]{2,1,0:T(8,128)(2,1)}), bf16[16,48,768]{2,1,0:T(8,128)(2,1)S(1)}, u32[]{:S(2)}, u32[]{:S(2)}) async-start(bf16[16,48,768]{2,1,0:T(8,128)(2,1)} %bitcast.8), calls=%async_computation.3 | async-start | bytes 2359296 | tf_op jit(solution)/shard_map/all_to_all | solution.py:80
Sparse Core Ops, SparseCore 0:
  10.5 57.6 all-gather.2
  173.1 133.5 all-reduce.1
